TPU v7x, 512 devices: a whole 4x4x16 slice. The times are simulated.
512 devices in a mesh: section: 2 (over core), dp: 64 (over z, x), mp: 4 (over y).
Axes of the slice: x: 4, y: 4, z: 16, core: 2. Of those that a mesh axis runs over, the one named last changes fastest.
Arguments:
- states: bfloat16 [512, 24, 4096], P('dp')
- norm_gain: float32 [4096], replicated, may hold values from 0.1 to 1.9
- key_weight: bfloat16 [4096, 4096], P('dp', ('section', 'mp')), may hold values from -0.09375 to 0.09375
- value_weight: bfloat16 [4096, 4096], P('dp', ('section', 'mp')), may hold values from -0.09375 to 0.09375
- pass_len: int32 [512], P('dp'), may hold values from 1 to 24
- retrieval: int32 [64, 64], replicated, may hold values from 0 to 511, as said below
- queries: bfloat16 [64, 32, 4096], P('dp', None, ('section', 'mp'))
Outputs:
- context: bfloat16 [64, 32, 4096], P('dp', None, ('section', 'mp'))
- passage_scores: float32 [64, 64], P('dp')
Inputs may be any that keep to these rules, and one draw needn't show every extreme that they name: `retrieval`: each question's list names 64 different passages. Counting passages of one block of 8 ids (the same id // 8), a list names passages of between 32 and 63 different blocks, at most 2 from any block, and exactly 2 from at least one. Popular passages recur in many lists.
All inputs are finite; a program needn't handle non-finite values.
Results may differ from a plain program's by a relative error of at most 0.013.
Values may be sent and summed in bfloat16 or wider, within the bound.
No kernel may reach another device: no remote copies, remote signals or barrier semaphores. Data moves between devices by JAX's collectives and lax.ppermute only.
A program may use at most 128 MiB of HBM per device.

v0:
```python
import jax
import jax.numpy as jnp
from jax import lax
from jax.sharding import PartitionSpec as P

HS = 64
WIRE = jnp.bfloat16


def _plane_shape(mesh):
    n_dp = mesh.shape["dp"]
    try:
        xs = {d.coords[0] for d in mesh.devices[0, :, 0]}
        nx = len(xs)
    except Exception:
        nx = 2 if n_dp % 2 == 0 else 1
    return (n_dp // nx, nx)


def _ring_perm(nz, nx, along, step):
    pairs = []
    for z in range(nz):
        for x in range(nx):
            if along == "x":
                dst = z * nx + (x + step) % nx
            else:
                dst = (z + step) % nz * nx + x
            pairs.append((z * nx + x, dst))
    return pairs


def _send(tree, perm):
    return jax.tree.map(lambda a: lax.ppermute(a, "dp", perm), tree)


def _gather_ring(block, n, fwd, bwd):
    if n == 1:
        return block[None]
    rel = [None] * n
    rel[0] = block
    f = block
    g = block
    for k in range(1, (n - 1) // 2 + 1):
        f = lax.ppermute(f, "dp", fwd)
        g = lax.ppermute(g, "dp", bwd)
        rel[n - k] = f
        rel[k] = g
    if n % 2 == 0:
        half = n // 2
        if block.shape[0] >= 2:
            cut = block.shape[0] // 2
            a = lax.ppermute(f[:cut], "dp", fwd)
            b = lax.ppermute(g[cut:], "dp", bwd)
            rel[half] = jnp.concatenate([a, b], axis=0)
        else:
            rel[half] = lax.ppermute(f, "dp", fwd)
    return jnp.stack(rel)


def _combine(a, b):
    ma, la, oa, ea = a
    mb, lb, ob, eb = b
    m = jnp.maximum(ma, mb)
    sa = jnp.where(ma == m, 1.0, jnp.exp(ma - m))
    sb = jnp.where(mb == m, 1.0, jnp.exp(mb - m))
    l = sa * la + sb * lb
    sa_o = jnp.swapaxes(sa, -1, -2)[..., None]
    sb_o = jnp.swapaxes(sb, -1, -2)[..., None]
    o = oa * sa_o + ob * sb_o
    e = ea * sa[..., None] + eb * sb[..., None]
    return (m, l, o, e)


def _to_wire(s):
    m, l, o, e = s
    return (m, l, o.astype(WIRE), e.astype(WIRE))


def _from_wire(s):
    m, l, o, e = s
    return (m, l, o.astype(jnp.float32), e.astype(jnp.float32))


def _reduce_ring(state, axis, me, n, fwd, bwd):

    def chunk(r):
        idx = (me + r) % n
        return jax.tree.map(lambda a: lax.dynamic_index_in_dim(a, idx, axis, keepdims=False), state)

    if n == 1:
        return chunk(0)
    nb = n // 2
    nf = n - 1 - nb
    bacc = chunk(n - nb)
    facc = None
    result = None
    for k in range(1, nb + 1):
        if nf > 0 and k == nb - nf + 1:
            facc = chunk(nf)
        recv_b = _from_wire(_send(_to_wire(bacc), bwd))
        recv_f = _from_wire(_send(_to_wire(facc), fwd)) if facc is not None else None
        if k < nb:
            bacc = _combine(recv_b, chunk((k - nb) % n))
            if recv_f is not None:
                facc = _combine(recv_f, chunk(nb - k))
        else:
            result = _combine(chunk(0), recv_b)
            if recv_f is not None:
                result = _combine(result, recv_f)
    return result


def _local(nz, nx, states, norm_gain, key_weight, value_weight, pass_len, retrieval, queries):
    blocks, tokens, model_width = states.shape
    inner = key_weight.shape[1]
    heads = inner // HS
    rows_here = key_weight.shape[0]
    n_dp = nz * nx
    dpi = lax.axis_index("dp")
    zi = dpi // nx
    xi = dpi % nx
    xf = _ring_perm(nz, nx, "x", 1)
    xb = _ring_perm(nz, nx, "x", -1)
    zf = _ring_perm(nz, nx, "z", 1)
    zb = _ring_perm(nz, nx, "z", -1)
    wkv = jnp.concatenate([key_weight, value_weight], axis=1)
    wx = _gather_ring(wkv, nx, xf, xb)
    wzx = _gather_ring(wx, nz, zf, zb)
    q_all = lax.all_gather(queries, "dp", axis=0, tiled=True)
    widened = states.astype(jnp.float32)
    mean_square = jnp.mean(widened * widened, axis=-1, keepdims=True)
    normed = (widened * lax.rsqrt(mean_square + 1e-06) * norm_gain).astype(jnp.bfloat16)
    flat = normed.reshape(blocks * tokens, nz, nx, rows_here)
    flat = jnp.roll(flat, -zi, axis=1)
    flat = jnp.roll(flat, -xi, axis=2)
    kv = jnp.dot(
        flat.reshape(blocks * tokens, model_width),
        wzx.reshape(model_width, 2 * inner),
        preferred_element_type=jnp.float32,
    ).astype(jnp.bfloat16)
    keys = kv[:, :inner].reshape(blocks, tokens, heads, HS)
    values = kv[:, inner:].reshape(blocks, tokens, heads, HS)
    n_q, answer_len, _ = q_all.shape
    q_heads = q_all.reshape(n_q, answer_len, heads, HS)
    scores = jnp.einsum("qthe,pshe->qhtps", q_heads, keys, preferred_element_type=jnp.float32)
    local_ids = retrieval - dpi * blocks
    owned = (local_ids >= 0) & (local_ids < blocks)
    onehot = (local_ids[:, None, :] == jnp.arange(blocks, dtype=jnp.int32)[None, :, None]) & owned[
        :, None, :
    ]
    picked = jnp.any(onehot, axis=2)
    positions = jnp.arange(tokens, dtype=jnp.int32)
    live = picked[:, :, None] & (positions[None, None, :] < pass_len[None, :, None])
    live5 = live[:, None, None, :, :]
    masked = jnp.where(live5, scores, -jnp.inf)
    m_loc = jnp.max(masked, axis=(3, 4))
    e = jnp.where(live5, jnp.exp(scores - m_loc[..., None, None]), 0.0)
    l_loc = jnp.sum(e, axis=(3, 4))
    e_pass = jnp.sum(e, axis=4)
    e_slot = jnp.einsum(
        "qhtp,qpj->qhtj", e_pass, onehot.astype(jnp.float32), precision=lax.Precision.HIGHEST
    )
    o_loc = jnp.einsum(
        "qhtps,pshe->qthe", e, values.astype(jnp.float32), precision=lax.Precision.HIGHEST
    )
    n_local_q = n_q // n_dp

    def split_q(a):
        return a.reshape((nz, nx, n_local_q) + a.shape[1:])

    state = jax.tree.map(split_q, (m_loc, l_loc, o_loc, e_slot))
    state = _reduce_ring(state, 1, xi, nx, xf, xb)
    state = _reduce_ring(state, 0, zi, nz, zf, zb)
    m_fin, l_fin, o_fin, e_fin = state
    context = o_fin / jnp.swapaxes(l_fin, -1, -2)[..., None]
    context = context.reshape(n_local_q, answer_len, inner).astype(jnp.bfloat16)
    mass = jnp.sum(e_fin / l_fin[..., None], axis=(1, 2)) / answer_len
    mass = lax.psum(mass, ("section", "mp"))
    return (context, mass)


def solution(mesh):
    nz, nx = _plane_shape(mesh)
    in_specs = (
        P("dp", None, None),
        P(),
        P("dp", ("section", "mp")),
        P("dp", ("section", "mp")),
        P("dp"),
        P(),
        P("dp", None, ("section", "mp")),
    )
    out_specs = (P("dp", None, ("section", "mp")), P("dp", None))

    def body(*args):
        return _local(nz, nx, *args)

    return jax.shard_map(body, mesh=mesh, in_specs=in_specs, out_specs=out_specs, check_vma=False)
```

profile of v0, /device:TPU:1, one launch (start us, length us, event | category | flops | bytes accessed | tf_op | source)
XLA Modules:
  0.0 677.8 jit_solution(13137495287411351185)
XLA Ops:
  25.1 11.3 %collective-permute-start.4 = (bf16[4,64,1024]{2,1,0:T(8,128)(2,1)S(1)}, bf16[4,64,1024]{2,1,0:T(8,128)(2,1)S(1)}, u32[]{:S(2)}, u32[]{:S(2)}) collective-permute-start(bf16[4,64,1024]{2,1,0:T(8,128)(2,1)S(1)} %pad_maximum_fusion), channel_id=1, source_target_pairs={{0,240},{4,244},{8,248},{12,252},{16,0},{20,4},{24,8},{28,12},{32,... | collective-permute-start | bytes 1572872 | tf_op jit(solution)/shard_map/ppermute | solution.py:45
  38.3 6.7 collective-permute-done.4
  45.0 5.3 collective-permute-start.5
  52.3 5.8 collective-permute-done.5
  58.0 5.4 collective-permute-start.6
  70.7 5.3 collective-permute-start.7
  83.9 4.7 copy.71
  91.3 4.6 collective-permute-start.8
  102.7 5.1 collective-permute-start.9
  114.8 4.9 collective-permute-start.10
  125.3 8.0 %collective-permute-done.17 = bf16[4,64,1024]{2,1,0:T(8,128)(2,1)S(1)} collective-permute-done((bf16[4,64,1024]{2,1,0:T(8,128)(2,1)S(1)}, bf16[4,64,1024]{2,1,0:T(8,128)(2,1)S(1)}, u32[]{:S(2)}, u32[]{:S(2)}) %collective-permute-start.17) | collective-permute-done | bytes 524320 | tf_op jit(solution)/shard_map/ppermute | solution.py:44
  139.9 4.8 collective-permute-done.18
  151.7 46.2 %all-gather.2.cloned.1.call-done = bf16[64,32,512]{2,1,0:T(8,128)(2,1)} async-done(((bf16[1,32,512]{2,1,0:T(8,128)(2,1)}), bf16[64,32,512]{2,1,0:T(8,128)(2,1)}) %all-gather.2.cloned.1.call-update) | async-done | bytes 2097168 | tf_op jit(solution)/shard_map/all_gather | solution.py:129
  197.8 6.7 reshape.804
  204.5 20.0 %fusion = (f32[64,8,32]{0,2,1:T(8,128)S(1)}, f32[8,8,24,64,32]{3,2,4,1,0:T(8,128)}) fusion(pred[64,8,24]{0,2,1:T(8,128)(4,1)S(1)} %broadcast_and_fusion, bf16[64,32,8,64,1]{3,2,1,0,4:T(8,128)(2,1)} %bitcast.753, bf16[8,24,8,64,1]{3,2,1,0,4:T(8,128)(2,1)S(1)} %bitcast.760), kind=kOutput, calls=%fused_computation.2 | convolution fusion | flops 408928256 | bytes 14954496 | tf_op jit(solution)/shard_map/qthe,pshe->qhtps/dot_general | solution.py:145
  224.7 22.8 %fusion.243 = (f32[64,8,32,8]{0,2,3,1:T(8,128)S(1)}, f32[64,8,32]{0,2,1:T(8,128)S(1)}, f32[64,8,32,8,24]{0,4,2,3,1:T(8,128)}) fusion(f32[64,8,32]{0,2,1:T(8,128)S(1)} %get-tuple-element.164, f32[8,8,24,64,32]{3,2,4,1,0:T(8,128)} %get-tuple-element.165, pred[64,8,24]{0,2,1:T(8,128)(4,1)S(1)} %broadcast_and_fusion), kind=kLoop, calls=%fused_computation.390 | loop fusion | flops 12435456 | bytes 25833472 | tf_op jit(solution)/shard_map/reduce_sum | solution.py:159
  270.2 4.8 collective-permute-start.27
  276.4 5.0 collective-permute-start.28
  282.8 4.8 collective-permute-start.29
  296.1 4.8 collective-permute-start.31
  333.7 7.5 %fusion.43 = f32[64,8,32,64]{3,2,1,0:T(8,128)S(1)} fusion(f32[64,8,32,8]{2,3,1,0:T(8,128)S(1)} %copy.118, s32[64,64]{1,0:T(8,128)} %copy-done.22, pred[64,64]{1,0:T(8,128)(4,1)S(1)} %get-tuple-element.71), kind=kOutput, calls=%fused_computation.70 | convolution fusion | flops 100728832 | bytes 4739072 | tf_op jit(solution)/shard_map/qhtp,qpj->qhtj/dot_general | solution.py:160
  362.7 16.9 %fusion.7 = f32[64,32,8,64]{0,3,1,2:T(8,128)} fusion(f32[64,8,32,8,24]{0,4,2,3,1:T(8,128)} %get-tuple-element.70, bf16[8,24,8,64,1]{3,2,1,0,4:T(8,128)(2,1)S(1)} %bitcast.759), kind=kOutput, calls=%fused_computation.15 | convolution fusion | flops 2415919104 | bytes 16973824 | tf_op jit(solution)/shard_map/qhtps,pshe->qthe/dot_general | solution.py:163
  379.6 9.8 %copy.78 = f32[64,32,8,64]{3,2,1,0:T(8,128)} copy(f32[64,32,8,64]{0,3,1,2:T(8,128)} %fusion.7) | data formatting | bytes 8388608 | tf_op jit(solution)/shard_map/qhtps,pshe->qthe/transpose | solution.py:163
  431.3 4.6 collective-permute-start.64
  520.1 4.7 collective-permute-start.34
  541.0 4.6 collective-permute-start.36
  583.9 4.6 collective-permute-start.39
  591.4 4.6 collective-permute-start.83
  598.2 4.6 collective-permute-start.40
  604.9 4.6 collective-permute-start.84
  611.7 4.6 collective-permute-start.41
  618.6 51.0 %psum.7 = f32[1,64]{1,0:T(1,128)} all-reduce(f32[1,64]{1,0:T(1,128)S(1)} %multiply_bitcast_fusion), channel_id=1, replica_groups=mesh['section'=2,'dp'=64,'mp'=4] {'section','mp'}, use_global_device_ids=true, to_apply=%region_6.7 | all-reduce | flops 64 | bytes 512 | tf_op jit(solution)/shard_map/psum | solution.py:178
  (521 shorter events, 351.0 us)
Async XLA Ops:
  7.2 190.7 %all-gather.2.cloned.1.call-start = ((), (), s32[]{:S(2)}) async-start(), calls=%async_computation | async-start | bytes 2129920 | tf_op jit(solution)/shard_map/all_gather | solution.py:129
  25.1 19.9 %collective-permute-start.4 = (bf16[4,64,1024]{2,1,0:T(8,128)(2,1)S(1)}, bf16[4,64,1024]{2,1,0:T(8,128)(2,1)S(1)}, u32[]{:S(2)}, u32[]{:S(2)}) collective-permute-start(bf16[4,64,1024]{2,1,0:T(8,128)(2,1)S(1)} %pad_maximum_fusion), channel_id=1, source_target_pairs={{0,240},{4,244},{8,248},{12,252},{16,0},{20,4},{24,8},{28,12},{32,... | collective-permute-start | bytes 1572872 | tf_op jit(solution)/shard_map/ppermute | solution.py:45
  70.7 20.6 %collective-permute-start.7 = (bf16[4,64,1024]{2,1,0:T(8,128)(2,1)}, bf16[4,64,1024]{2,1,0:T(8,128)(2,1)}, u32[]{:S(2)}, u32[]{:S(2)}) collective-permute-start(bf16[4,64,1024]{2,1,0:T(8,128)(2,1)} %collective-permute-done.6), channel_id=1, source_target_pairs={{0,240},{4,244},{8,248},{12,252},{16,0},{20,4},{24,8},{28,12},{32,... | collective-permute-start | bytes 1572872 | tf_op jit(solution)/shard_map/ppermute | solution.py:45
  76.0 19.9 %collective-permute-start.14 = (bf16[4,64,1024]{2,1,0:T(8,128)(2,1)}, bf16[4,64,1024]{2,1,0:T(8,128)(2,1)}, u32[]{:S(2)}, u32[]{:S(2)}) collective-permute-start(bf16[4,64,1024]{2,1,0:T(8,128)(2,1)} %collective-permute-done.13), channel_id=1, source_target_pairs={{0,16},{4,20},{8,24},{12,28},{16,32},{20,36},{24,40},{28,44},{32,4... | collective-permute-start | bytes 1572872 | tf_op jit(solution)/shard_map/ppermute | solution.py:44
  114.8 20.4 %collective-permute-start.10 = (bf16[4,64,1024]{2,1,0:T(8,128)(2,1)S(1)}, bf16[4,64,1024]{2,1,0:T(8,128)(2,1)S(1)}, u32[]{:S(2)}, u32[]{:S(2)}) collective-permute-start(bf16[4,64,1024]{2,1,0:T(8,128)(2,1)S(1)} %collective-permute-done.9), channel_id=1, source_target_pairs={{0,240},{4,244},{8,248},{12,252},{16,0},{20,4},{24,8},{28,12},{32,... | collective-permute-start | bytes 1572872 | tf_op jit(solution)/shard_map/ppermute | solution.py:45
  322.4 21.0 %collective-permute-start.33 = (f32[1,8,32]{2,1,0:T(8,128)S(1)}, f32[1,8,32]{2,1,0:T(8,128)S(1)}, u32[]{:S(2)}, u32[]{:S(2)}) collective-permute-start(f32[1,8,32]{2,1,0:T(8,128)S(1)} %get-tuple-element.7), channel_id=1, source_target_pairs={{0,240},{4,244},{8,248},{12,252},{16,0},{20,4},{24,8},{28,12},{32,... | collective-permute-start | bytes 3080 | tf_op jit(solution)/shard_map/ppermute | solution.py:33
  325.5 17.9 %collective-permute-start.45 = (f32[1,8,32]{2,1,0:T(8,128)S(1)}, f32[1,8,32]{2,1,0:T(8,128)S(1)}, u32[]{:S(2)}, u32[]{:S(2)}) collective-permute-start(f32[1,8,32]{2,1,0:T(8,128)S(1)} %get-tuple-element.133), channel_id=1, source_target_pairs={{0,16},{4,20},{8,24},{12,28},{16,32},{20,36},{24,40},{28,44},{32,4... | collective-permute-start | bytes 3080 | tf_op jit(solution)/shard_map/ppermute | solution.py:33
  329.4 14.1 %collective-permute-start.59 = (f32[1,8,32]{2,1,0:T(8,128)S(1)}, f32[1,8,32]{2,1,0:T(8,128)S(1)}, u32[]{:S(2)}, u32[]{:S(2)}) collective-permute-start(f32[1,8,32]{2,1,0:T(8,128)S(1)} %get-tuple-element.144), channel_id=1, source_target_pairs={{0,240},{4,244},{8,248},{12,252},{16,0},{20,4},{24,8},{28,12},{32,... | collective-permute-start | bytes 3080 | tf_op jit(solution)/shard_map/ppermute | solution.py:33
  341.3 14.5 %collective-permute-start.67 = (f32[1,8,32]{2,1,0:T(8,128)S(1)}, f32[1,8,32]{2,1,0:T(8,128)S(1)}, u32[]{:S(2)}, u32[]{:S(2)}) collective-permute-start(f32[1,8,32]{2,1,0:T(8,128)S(1)} %get-tuple-element.145), channel_id=1, source_target_pairs={{0,16},{4,20},{8,24},{12,28},{16,32},{20,36},{24,40},{28,44},{32,4... | collective-permute-start | bytes 3080 | tf_op jit(solution)/shard_map/ppermute | solution.py:33
  350.3 126.9 %collective-permute-start.74 = (bf16[16,1,8,32,64]{4,3,2,0,1:T(8,128)(2,1)}, bf16[16,1,8,32,64]{4,3,2,0,1:T(8,128)(2,1)S(1)}, u32[]{:S(2)}, u32[]{:S(2)}) collective-permute-start(bf16[16,1,8,32,64]{4,3,2,0,1:T(8,128)(2,1)} %get-tuple-element.73), channel_id=1, source_target_pairs={{0,12},{4,0},{8,4},{12,8},{16,28},{20,16},{24,20},{28,24},{32,44},... | collective-permute-start | bytes 1572872 | tf_op jit(solution)/shard_map/ppermute | solution.py:33
  352.2 149.5 %collective-permute-start.76 = (bf16[16,1,8,32,64]{4,3,2,0,1:T(8,128)(2,1)S(1)}, bf16[16,1,8,32,64]{4,3,2,0,1:T(8,128)(2,1)}, u32[]{:S(2)}, u32[]{:S(2)}) collective-permute-start(bf16[16,1,8,32,64]{4,3,2,0,1:T(8,128)(2,1)S(1)} %get-tuple-element.74), channel_id=1, source_target_pairs={{0,4},{4,8},{8,12},{12,0},{16,20},{20,24},{24,28},{28,16},{32,36},... | collective-permute-start | bytes 1572872 | tf_op jit(solution)/shard_map/ppermute | solution.py:33
  357.2 32.2 %collective-permute-start.61 = (f32[1,8,32]{2,1,0:T(8,128)S(1)}, f32[1,8,32]{2,1,0:T(8,128)S(1)}, u32[]{:S(2)}, u32[]{:S(2)}) collective-permute-start(f32[1,8,32]{2,1,0:T(8,128)S(1)} %get-tuple-element.50), channel_id=1, source_target_pairs={{0,240},{4,244},{8,248},{12,252},{16,0},{20,4},{24,8},{28,12},{32,... | collective-permute-start | bytes 3080 | tf_op jit(solution)/shard_map/ppermute | solution.py:33
  359.1 30.3 %collective-permute-start.68 = (f32[1,8,32]{2,1,0:T(8,128)S(1)}, f32[1,8,32]{2,1,0:T(8,128)S(1)}, u32[]{:S(2)}, u32[]{:S(2)}) collective-permute-start(f32[1,8,32]{2,1,0:T(8,128)S(1)} %get-tuple-element.126), channel_id=1, source_target_pairs={{0,16},{4,20},{8,24},{12,28},{16,32},{20,36},{24,40},{28,44},{32,4... | collective-permute-start | bytes 3080 | tf_op jit(solution)/shard_map/ppermute | solution.py:33
  390.8 20.0 %collective-permute-start.62 = (f32[1,8,32]{2,1,0:T(8,128)}, f32[1,8,32]{2,1,0:T(8,128)S(1)}, u32[]{:S(2)}, u32[]{:S(2)}) collective-permute-start(f32[1,8,32]{2,1,0:T(8,128)} %get-tuple-element.48), channel_id=1, source_target_pairs={{0,240},{4,244},{8,248},{12,252},{16,0},{20,4},{24,8},{28,12},{32,... | collective-permute-start | bytes 3080 | tf_op jit(solution)/shard_map/ppermute | solution.py:33
  393.9 17.5 %collective-permute-start.69 = (f32[1,8,32]{2,1,0:T(8,128)}, f32[1,8,32]{2,1,0:T(8,128)}, u32[]{:S(2)}, u32[]{:S(2)}) collective-permute-start(f32[1,8,32]{2,1,0:T(8,128)} %get-tuple-element.124), channel_id=1, source_target_pairs={{0,16},{4,20},{8,24},{12,28},{16,32},{20,36},{24,40},{28,44},{32,4... | collective-permute-start | bytes 3080 | tf_op jit(solution)/shard_map/ppermute | solution.py:33
  408.2 19.8 %collective-permute-start.46 = (f32[1,8,32]{2,1,0:T(8,128)}, f32[1,8,32]{2,1,0:T(8,128)}, u32[]{:S(2)}, u32[]{:S(2)}) collective-permute-start(f32[1,8,32]{2,1,0:T(8,128)} %get-tuple-element.131), channel_id=1, source_target_pairs={{0,16},{4,20},{8,24},{12,28},{16,32},{20,36},{24,40},{28,44},{32,4... | collective-permute-start | bytes 3080 | tf_op jit(solution)/shard_map/ppermute | solution.py:33
  412.8 15.3 %collective-permute-start.63 = (f32[1,8,32]{2,1,0:T(8,128)}, f32[1,8,32]{2,1,0:T(8,128)}, u32[]{:S(2)}, u32[]{:S(2)}) collective-permute-start(f32[1,8,32]{2,1,0:T(8,128)} %get-tuple-element.46), channel_id=1, source_target_pairs={{0,240},{4,244},{8,248},{12,252},{16,0},{20,4},{24,8},{28,12},{32,... | collective-permute-start | bytes 3080 | tf_op jit(solution)/shard_map/ppermute | solution.py:33
  429.4 15.9 %collective-permute-start.47 = (f32[1,8,32]{2,1,0:T(8,128)}, f32[1,8,32]{2,1,0:T(8,128)S(1)}, u32[]{:S(2)}, u32[]{:S(2)}) collective-permute-start(f32[1,8,32]{2,1,0:T(8,128)} %get-tuple-element.139), channel_id=1, source_target_pairs={{0,16},{4,20},{8,24},{12,28},{16,32},{20,36},{24,40},{28,44},{32,4... | collective-permute-start | bytes 3080 | tf_op jit(solution)/shard_map/ppermute | solution.py:33
  431.3 17.1 %collective-permute-start.64 = (f32[1,8,32]{2,1,0:T(8,128)}, f32[1,8,32]{2,1,0:T(8,128)}, u32[]{:S(2)}, u32[]{:S(2)}) collective-permute-start(f32[1,8,32]{2,1,0:T(8,128)} %get-tuple-element.44), channel_id=1, source_target_pairs={{0,240},{4,244},{8,248},{12,252},{16,0},{20,4},{24,8},{28,12},{32,... | collective-permute-start | bytes 3080 | tf_op jit(solution)/shard_map/ppermute | solution.py:33
  445.3 51.9 %collective-permute-start.22 = (bf16[16,1,32,8,64]{4,3,2,0,1:T(8,128)(2,1)}, bf16[16,1,32,8,64]{4,3,2,0,1:T(8,128)(2,1)}, u32[]{:S(2)}, u32[]{:S(2)}) collective-permute-start(bf16[16,1,32,8,64]{4,3,2,0,1:T(8,128)(2,1)} %get-tuple-element.75), channel_id=1, source_target_pairs={{0,12},{4,0},{8,4},{12,8},{16,28},{20,16},{24,20},{28,24},{32,44},... | collective-permute-start | bytes 1572872 | tf_op jit(solution)/shard_map/ppermute | solution.py:33
  449.8 14.6 %collective-permute-start.65 = (f32[1,8,32]{2,1,0:T(8,128)}, f32[1,8,32]{2,1,0:T(8,128)}, u32[]{:S(2)}, u32[]{:S(2)}) collective-permute-start(f32[1,8,32]{2,1,0:T(8,128)} %get-tuple-element.42), channel_id=1, source_target_pairs={{0,240},{4,244},{8,248},{12,252},{16,0},{20,4},{24,8},{28,12},{32,... | collective-permute-start | bytes 3080 | tf_op jit(solution)/shard_map/ppermute | solution.py:33
  464.4 17.9 %collective-permute-start.48 = (f32[1,8,32]{2,1,0:T(8,128)}, f32[1,8,32]{2,1,0:T(8,128)}, u32[]{:S(2)}, u32[]{:S(2)}) collective-permute-start(f32[1,8,32]{2,1,0:T(8,128)} %get-tuple-element.135), channel_id=1, source_target_pairs={{0,16},{4,20},{8,24},{12,28},{16,32},{20,36},{24,40},{28,44},{32,4... | collective-permute-start | bytes 3080 | tf_op jit(solution)/shard_map/ppermute | solution.py:33
  467.7 16.9 %collective-permute-start.66 = (f32[1,8,32]{2,1,0:T(8,128)}, f32[1,8,32]{2,1,0:T(8,128)}, u32[]{:S(2)}, u32[]{:S(2)}) collective-permute-start(f32[1,8,32]{2,1,0:T(8,128)} %get-tuple-element.40), channel_id=1, source_target_pairs={{0,240},{4,244},{8,248},{12,252},{16,0},{20,4},{24,8},{28,12},{32,... | collective-permute-start | bytes 3080 | tf_op jit(solution)/shard_map/ppermute | solution.py:33
  482.4 30.6 %collective-permute-start.25 = (bf16[16,1,32,8,64]{4,3,2,0,1:T(8,128)(2,1)S(1)}, bf16[16,1,32,8,64]{4,3,2,0,1:T(8,128)(2,1)}, u32[]{:S(2)}, u32[]{:S(2)}) collective-permute-start(bf16[16,1,32,8,64]{4,3,2,0,1:T(8,128)(2,1)S(1)} %get-tuple-element.76), channel_id=1, source_target_pairs={{0,4},{4,8},{8,12},{12,0},{16,20},{20,24},{24,28},{28,16},{32,36},... | collective-permute-start | bytes 1572872 | tf_op jit(solution)/shard_map/ppermute | solution.py:33
  484.7 17.1 %collective-permute-start.75 = (bf16[16,1,8,32,64]{4,3,2,0,1:T(8,128)(2,1)}, bf16[16,1,8,32,64]{4,3,2,0,1:T(8,128)(2,1)S(1)}, u32[]{:S(2)}, u32[]{:S(2)}) collective-permute-start(bf16[16,1,8,32,64]{4,3,2,0,1:T(8,128)(2,1)} %fusion.18), channel_id=1, source_target_pairs={{0,12},{4,0},{8,4},{12,8},{16,28},{20,16},{24,20},{28,24},{32,44},... | collective-permute-start | bytes 1572872 | tf_op jit(solution)/shard_map/ppermute | solution.py:33
  499.8 15.9 %collective-permute-start.23 = (bf16[16,1,32,8,64]{4,3,2,0,1:T(8,128)(2,1)S(1)}, bf16[16,1,32,8,64]{4,3,2,0,1:T(8,128)(2,1)S(1)}, u32[]{:S(2)}, u32[]{:S(2)}) collective-permute-start(bf16[16,1,32,8,64]{4,3,2,0,1:T(8,128)(2,1)S(1)} %fusion.23), channel_id=1, source_target_pairs={{0,12},{4,0},{8,4},{12,8},{16,28},{20,16},{24,20},{28,24},{32,44},... | collective-permute-start | bytes 1572872 | tf_op jit(solution)/shard_map/ppermute | solution.py:33
  506.1 27.5 %collective-permute-start.85 = (bf16[1,8,32,64]{3,2,1,0:T(8,128)(2,1)S(1)}, bf16[1,8,32,64]{3,2,1,0:T(8,128)(2,1)S(1)}, u32[]{:S(2)}, u32[]{:S(2)}) collective-permute-start(bf16[1,8,32,64]{3,2,1,0:T(8,128)(2,1)S(1)} %fusion.112), channel_id=1, source_target_pairs={{0,16},{4,20},{8,24},{12,28},{16,32},{20,36},{24,40},{28,44},{32,4... | collective-permute-start | bytes 98312 | tf_op jit(solution)/shard_map/ppermute | solution.py:33
  508.5 18.3 %collective-permute-start.77 = (bf16[1,8,32,64]{3,2,1,0:T(8,128)(2,1)S(1)}, bf16[1,8,32,64]{3,2,1,0:T(8,128)(2,1)S(1)}, u32[]{:S(2)}, u32[]{:S(2)}) collective-permute-start(bf16[1,8,32,64]{3,2,1,0:T(8,128)(2,1)S(1)} %fusion.111), channel_id=1, source_target_pairs={{0,240},{4,244},{8,248},{12,252},{16,0},{20,4},{24,8},{28,12},{32,... | collective-permute-start | bytes 98312 | tf_op jit(solution)/shard_map/ppermute | solution.py:33
  524.8 15.8 %collective-permute-start.49 = (bf16[1,32,8,64]{3,2,1,0:T(8,128)(2,1)S(1)}, bf16[1,32,8,64]{3,2,1,0:T(8,128)(2,1)S(1)}, u32[]{:S(2)}, u32[]{:S(2)}) collective-permute-start(bf16[1,32,8,64]{3,2,1,0:T(8,128)(2,1)S(1)} %get-tuple-element.102), channel_id=1, source_target_pairs={{0,16},{4,20},{8,24},{12,28},{16,32},{20,36},{24,40},{28,44},{32,4... | collective-permute-start | bytes 98312 | tf_op jit(solution)/shard_map/ppermute | solution.py:33
  569.5 14.2 %collective-permute-start.38 = (bf16[1,32,8,64]{3,2,1,0:T(8,128)(2,1)S(1)}, bf16[1,32,8,64]{3,2,1,0:T(8,128)(2,1)S(1)}, u32[]{:S(2)}, u32[]{:S(2)}) collective-permute-start(bf16[1,32,8,64]{3,2,1,0:T(8,128)(2,1)S(1)} %get-tuple-element.95), channel_id=1, source_target_pairs={{0,240},{4,244},{8,248},{12,252},{16,0},{20,4},{24,8},{28,12},{32,... | collective-permute-start | bytes 98312 | tf_op jit(solution)/shard_map/ppermute | solution.py:33
  611.7 57.9 %collective-permute-start.41 = (bf16[1,32,8,64]{3,2,1,0:T(8,128)(2,1)S(1)}, bf16[1,32,8,64]{3,2,1,0:T(8,128)(2,1)S(1)}, u32[]{:S(2)}, u32[]{:S(2)}) collective-permute-start(bf16[1,32,8,64]{3,2,1,0:T(8,128)(2,1)S(1)} %get-tuple-element.89), channel_id=1, source_target_pairs={{0,240},{4,244},{8,248},{12,252},{16,0},{20,4},{24,8},{28,12},{32,... | collective-permute-start | bytes 98312 | tf_op jit(solution)/shard_map/ppermute | solution.py:33
  616.3 53.3 %collective-permute-start.55 = (bf16[1,32,8,64]{3,2,1,0:T(8,128)(2,1)S(1)}, bf16[1,32,8,64]{3,2,1,0:T(8,128)(2,1)S(1)}, u32[]{:S(2)}, u32[]{:S(2)}) collective-permute-start(bf16[1,32,8,64]{3,2,1,0:T(8,128)(2,1)S(1)} %get-tuple-element.90), channel_id=1, source_target_pairs={{0,16},{4,20},{8,24},{12,28},{16,32},{20,36},{24,40},{28,44},{32,4... | collective-permute-start | bytes 98312 | tf_op jit(solution)/shard_map/ppermute | solution.py:33
  (176 other events, 5351.2 us)
Sparse Core Ops, SparseCore 0:
  65.6 132.2 all-gather.1
where the time goes:
time: 690 us; the launch traced here: 678 us
  starting transfers between devices  303 us (44%)
  waiting for transfers between devices  96.9 us (14%)
  local copies, waits for them, and re-layouts  91.3 us (13%)
  other arithmetic  70.6 us (10%)
  blocking collectives  51 us (7%)
  matrix products  46.9 us (7%)
  between operations  17.8 us (3%)
    ppermute x72, starting transfers between devices, _send(): return jax.tree.map(lambda a: lax.ppermute(a, 'dp', perm), tree)  228 us
    psum x1, blocking collectives, _local(): mass = lax.psum(mass, ('section', 'mp'))  51 us
    all_gather x1, waiting for transfers between devices, _local(): q_all = lax.all_gather(queries, 'dp', axis=0, tiled=True)  46.2 us
    ppermute x8, starting transfers between devices, _gather_ring(): g = lax.ppermute(g, 'dp', bwd)  45.1 us
    mul x36, local copies, waits for them, and re-layouts, _combine(): o = oa * sa_o + ob * sb_o  43.7 us
    ppermute x8, waiting for transfers between devices, _gather_ring(): g = lax.ppermute(g, 'dp', bwd)  23 us
    reduce_sum x1, other arithmetic, _local(): e_pass = jnp.sum(e, axis=4)  22.8 us
    dot_general x1, matrix products, _local(): jnp.einsum('qthe,pshe->qhtps', q_heads, keys, preferred_element_type=jnp....  20 us
  transfers between devices with their start and end apart: 93, of which 20 were waited for; matrix products, arithmetic and copies ran while one was open for 22% of the time, Pallas kernels for 0%

commit v1 on v0

--- a/solution.py
+++ b/solution.py
@@ -126,7 +126,9 @@
     wkv = jnp.concatenate([key_weight, value_weight], axis=1)
     wx = _gather_ring(wkv, nx, xf, xb)
     wzx = _gather_ring(wx, nz, zf, zb)
-    q_all = lax.all_gather(queries, "dp", axis=0, tiled=True)
+    q_all = jnp.concatenate(
+        lax.all_to_all(jnp.stack([queries] * lax.axis_size("dp")), "dp", 0, 0), axis=0
+    )
     widened = states.astype(jnp.float32)
     mean_square = jnp.mean(widened * widened, axis=-1, keepdims=True)
     normed = (widened * lax.rsqrt(mean_square + 1e-06) * norm_gain).astype(jnp.bfloat16)

time: 690 us -> 723 us (1.048)
  the two profiles are of different devices: /device:TPU:1 before, /device:TPU:97 now
where the time goes in v1:
time: 723 us; the launch traced here: 710 us
  starting transfers between devices  301 us (42%)
  waiting for transfers between devices  153 us (21%)
  local copies, waits for them, and re-layouts  91.4 us (13%)
  other arithmetic  67.3 us (9%)
  matrix products  46.8 us (6%)
  blocking collectives  46.3 us (6%)
    ppermute x72, starting transfers between devices, _send(): return jax.tree.map(lambda a: lax.ppermute(a, 'dp', perm), tree)  220 us
    ppermute x8, waiting for transfers between devices, _gather_ring(): g = lax.ppermute(g, 'dp', bwd)  116 us
    psum x1, blocking collectives, _local(): mass = lax.psum(mass, ('section', 'mp'))  46.3 us
    mul x36, local copies, waits for them, and re-layouts, _combine(): o = oa * sa_o + ob * sb_o  41.9 us
    ppermute x8, starting transfers between devices, _gather_ring(): f = lax.ppermute(f, 'dp', fwd)  35 us
    ppermute x72, waiting for transfers between devices, _send(): return jax.tree.map(lambda a: lax.ppermute(a, 'dp', perm), tree)  25.8 us
    reduce_sum x1, other arithmetic, _local(): e_pass = jnp.sum(e, axis=4)  22.8 us
    dot_general x1, matrix products, _local(): jnp.einsum('qthe,pshe->qhtps', q_heads, keys, preferred_element_type=jnp....  20 us
  transfers between devices with their start and end apart: 93, of which 19 were waited for; matrix products, arithmetic and copies ran while one was open for 21% of the time, Pallas kernels for 0%

profile of v1, /device:TPU:97, one launch (start us, length us, event | category | flops | bytes accessed | tf_op | source)
XLA Modules:
  0.0 710.3 jit_solution(11707269707214116594)
XLA Ops:
  11.8 4.6 collective-permute-start.3
  19.7 4.8 collective-permute-start.11
  26.9 15.9 %all-to-all-start = ((bf16[64,1,32,512]{3,2,1,0:T(8,128)(2,1)}), bf16[64,1,32,512]{3,2,1,0:T(8,128)(2,1)}, u32[]{:S(2)}, u32[]{:S(2)}) async-start(bf16[64,1,32,512]{3,2,1,0:T(8,128)(2,1)} %stack.68), calls=%async_computation | async-start | bytes 4194304 | tf_op jit(solution)/shard_map/all_to_all | solution.py:130
  49.4 96.6 %collective-permute-done.5 = bf16[4,64,1024]{2,1,0:T(8,128)(2,1)S(1)} collective-permute-done((bf16[4,64,1024]{2,1,0:T(8,128)(2,1)S(1)}, bf16[4,64,1024]{2,1,0:T(8,128)(2,1)S(1)}, u32[]{:S(2)}, u32[]{:S(2)}) %collective-permute-start.5) | collective-permute-done | bytes 524320 | tf_op jit(solution)/shard_map/ppermute | solution.py:45
  147.9 4.6 collective-permute-start.13
  152.9 8.1 %collective-permute-done.6 = bf16[4,64,1024]{2,1,0:T(8,128)(2,1)} collective-permute-done((bf16[4,64,1024]{2,1,0:T(8,128)(2,1)S(1)}, bf16[4,64,1024]{2,1,0:T(8,128)(2,1)}, u32[]{:S(2)}, u32[]{:S(2)}) %collective-permute-start.6) | collective-permute-done | bytes 524320 | tf_op jit(solution)/shard_map/ppermute | solution.py:45
  162.9 4.6 collective-permute-start.14
  173.5 4.8 copy.71
  182.8 4.6 collective-permute-start.15
  188.8 5.8 collective-permute-done.8
  202.3 5.1 collective-permute-done.9
  220.1 5.4 collective-permute-start.18
  228.7 5.1 collective-permute-done.19
  240.1 6.7 reshape_reshape.3
  246.7 20.0 %fusion = (f32[64,8,32]{0,2,1:T(8,128)S(1)}, f32[8,8,24,64,32]{3,2,4,1,0:T(8,128)}) fusion(pred[64,8,24]{0,2,1:T(8,128)(4,1)S(1)} %broadcast_and_fusion, bf16[64,32,8,64,1]{3,2,1,0,4:T(8,128)(2,1)} %bitcast.756, bf16[8,24,8,64,1]{3,2,1,0,4:T(8,128)(2,1)S(1)} %bitcast.763), kind=kOutput, calls=%fused_computation.2 | convolution fusion | flops 408928256 | bytes 14954496 | tf_op jit(solution)/shard_map/qthe,pshe->qhtps/dot_general | solution.py:147
  266.9 22.8 %fusion.243 = (f32[64,8,32,8]{0,2,3,1:T(8,128)S(1)}, f32[64,8,32]{0,2,1:T(8,128)S(1)}, f32[64,8,32,8,24]{0,4,2,3,1:T(8,128)}) fusion(f32[64,8,32]{0,2,1:T(8,128)S(1)} %get-tuple-element.164, f32[8,8,24,64,32]{3,2,4,1,0:T(8,128)} %get-tuple-element.165, pred[64,8,24]{0,2,1:T(8,128)(4,1)S(1)} %broadcast_and_fusion), kind=kLoop, calls=%fused_computation.390 | loop fusion | flops 12435456 | bytes 25833472 | tf_op jit(solution)/shard_map/reduce_sum | solution.py:161
  328.5 4.6 collective-permute-start.42
  341.8 4.6 collective-permute-start.43
  349.6 5.0 collective-permute-start.44
  375.7 7.5 %fusion.43 = f32[64,8,32,64]{3,2,1,0:T(8,128)S(1)} fusion(f32[64,8,32,8]{2,3,1,0:T(8,128)S(1)} %copy.118, s32[64,64]{1,0:T(8,128)} %copy-done.21, pred[64,64]{1,0:T(8,128)(4,1)S(1)} %get-tuple-element.71), kind=kOutput, calls=%fused_computation.70 | convolution fusion | flops 100728832 | bytes 4739072 | tf_op jit(solution)/shard_map/qhtp,qpj->qhtj/dot_general | solution.py:162
  383.3 4.7 collective-permute-start.67
  400.2 4.8 collective-permute-start.68
  405.0 16.9 %fusion.7 = f32[64,32,8,64]{0,3,1,2:T(8,128)} fusion(f32[64,8,32,8,24]{0,4,2,3,1:T(8,128)} %get-tuple-element.70, bf16[8,24,8,64,1]{3,2,1,0,4:T(8,128)(2,1)S(1)} %bitcast.762), kind=kOutput, calls=%fused_computation.15 | convolution fusion | flops 2415919104 | bytes 16973824 | tf_op jit(solution)/shard_map/qhtps,pshe->qthe/dot_general | solution.py:165
  421.8 9.8 %copy.78 = f32[64,32,8,64]{3,2,1,0:T(8,128)} copy(f32[64,32,8,64]{0,3,1,2:T(8,128)} %fusion.7) | data formatting | bytes 8388608 | tf_op jit(solution)/shard_map/qhtps,pshe->qthe/transpose | solution.py:165
  434.9 4.6 collective-permute-start.69
  479.5 4.6 collective-permute-start.71
  498.0 4.6 collective-permute-start.72
  587.8 4.6 collective-permute-start.50
  595.2 4.6 collective-permute-start.87
  602.0 4.6 collective-permute-start.51
  616.2 4.8 collective-permute-start.52
  662.7 46.3 %psum.7 = f32[1,64]{1,0:T(1,128)} all-reduce(f32[1,64]{1,0:T(1,128)S(1)} %multiply_bitcast_fusion), channel_id=1, replica_groups=mesh['section'=2,'dp'=64,'mp'=4] {'section','mp'}, use_global_device_ids=true, to_apply=%region_6.7 | all-reduce | flops 64 | bytes 512 | tf_op jit(solution)/shard_map/psum | solution.py:180
  (517 shorter events, 350.5 us)
Async XLA Ops:
  17.7 25.1 %collective-permute-start.4 = (bf16[4,64,1024]{2,1,0:T(8,128)(2,1)S(1)}, bf16[4,64,1024]{2,1,0:T(8,128)(2,1)S(1)}, u32[]{:S(2)}, u32[]{:S(2)}) collective-permute-start(bf16[4,64,1024]{2,1,0:T(8,128)(2,1)S(1)} %pad_maximum_fusion), channel_id=1, source_target_pairs={{0,240},{4,244},{8,248},{12,252},{16,0},{20,4},{24,8},{28,12},{32,... | collective-permute-start | bytes 1572872 | tf_op jit(solution)/shard_map/ppermute | solution.py:45
  19.7 25.4 %collective-permute-start.11 = (bf16[4,64,1024]{2,1,0:T(8,128)(2,1)S(1)}, bf16[4,64,1024]{2,1,0:T(8,128)(2,1)S(1)}, u32[]{:S(2)}, u32[]{:S(2)}) collective-permute-start(bf16[4,64,1024]{2,1,0:T(8,128)(2,1)S(1)} %pad_maximum_fusion), channel_id=1, source_target_pairs={{0,16},{4,20},{8,24},{12,28},{16,32},{20,36},{24,40},{28,44},{32,4... | collective-permute-start | bytes 1572872 | tf_op jit(solution)/shard_map/ppermute | solution.py:44
  26.9 213.1 %all-to-all-start = ((bf16[64,1,32,512]{3,2,1,0:T(8,128)(2,1)}), bf16[64,1,32,512]{3,2,1,0:T(8,128)(2,1)}, u32[]{:S(2)}, u32[]{:S(2)}) async-start(bf16[64,1,32,512]{3,2,1,0:T(8,128)(2,1)} %stack.68), calls=%async_computation | async-start | bytes 4194304 | tf_op jit(solution)/shard_map/all_to_all | solution.py:130
  42.9 103.1 %collective-permute-start.5 = (bf16[4,64,1024]{2,1,0:T(8,128)(2,1)S(1)}, bf16[4,64,1024]{2,1,0:T(8,128)(2,1)S(1)}, u32[]{:S(2)}, u32[]{:S(2)}) collective-permute-start(bf16[4,64,1024]{2,1,0:T(8,128)(2,1)S(1)} %collective-permute-done.4), channel_id=1, source_target_pairs={{0,240},{4,244},{8,248},{12,252},{16,0},{20,4},{24,8},{28,12},{32,... | collective-permute-start | bytes 1572872 | tf_op jit(solution)/shard_map/ppermute | solution.py:45
  45.1 102.8 %collective-permute-start.12 = (bf16[4,64,1024]{2,1,0:T(8,128)(2,1)S(1)}, bf16[4,64,1024]{2,1,0:T(8,128)(2,1)S(1)}, u32[]{:S(2)}, u32[]{:S(2)}) collective-permute-start(bf16[4,64,1024]{2,1,0:T(8,128)(2,1)S(1)} %collective-permute-done.11), channel_id=1, source_target_pairs={{0,16},{4,20},{8,24},{12,28},{16,32},{20,36},{24,40},{28,44},{32,4... | collective-permute-start | bytes 1572872 | tf_op jit(solution)/shard_map/ppermute | solution.py:44
  161.0 19.8 %collective-permute-start.7 = (bf16[4,64,1024]{2,1,0:T(8,128)(2,1)}, bf16[4,64,1024]{2,1,0:T(8,128)(2,1)}, u32[]{:S(2)}, u32[]{:S(2)}) collective-permute-start(bf16[4,64,1024]{2,1,0:T(8,128)(2,1)} %collective-permute-done.6), channel_id=1, source_target_pairs={{0,240},{4,244},{8,248},{12,252},{16,0},{20,4},{24,8},{28,12},{32,... | collective-permute-start | bytes 1572872 | tf_op jit(solution)/shard_map/ppermute | solution.py:45
  162.9 19.9 %collective-permute-start.14 = (bf16[4,64,1024]{2,1,0:T(8,128)(2,1)}, bf16[4,64,1024]{2,1,0:T(8,128)(2,1)}, u32[]{:S(2)}, u32[]{:S(2)}) collective-permute-start(bf16[4,64,1024]{2,1,0:T(8,128)(2,1)} %collective-permute-done.13), channel_id=1, source_target_pairs={{0,16},{4,20},{8,24},{12,28},{16,32},{20,36},{24,40},{28,44},{32,4... | collective-permute-start | bytes 1572872 | tf_op jit(solution)/shard_map/ppermute | solution.py:44
  207.4 18.0 %collective-permute-start.10 = (bf16[4,64,1024]{2,1,0:T(8,128)(2,1)S(1)}, bf16[4,64,1024]{2,1,0:T(8,128)(2,1)S(1)}, u32[]{:S(2)}, u32[]{:S(2)}) collective-permute-start(bf16[4,64,1024]{2,1,0:T(8,128)(2,1)S(1)} %collective-permute-done.9), channel_id=1, source_target_pairs={{0,240},{4,244},{8,248},{12,252},{16,0},{20,4},{24,8},{28,12},{32,... | collective-permute-start | bytes 1572872 | tf_op jit(solution)/shard_map/ppermute | solution.py:45
  347.7 16.4 %collective-permute-start.32 = (f32[1,8,32]{2,1,0:T(8,128)}, f32[1,8,32]{2,1,0:T(8,128)S(1)}, u32[]{:S(2)}, u32[]{:S(2)}) collective-permute-start(f32[1,8,32]{2,1,0:T(8,128)} %get-tuple-element.9), channel_id=1, source_target_pairs={{0,240},{4,244},{8,248},{12,252},{16,0},{20,4},{24,8},{28,12},{32,... | collective-permute-start | bytes 3080 | tf_op jit(solution)/shard_map/ppermute | solution.py:33
  365.4 22.6 %collective-permute-start.33 = (f32[1,8,32]{2,1,0:T(8,128)S(1)}, f32[1,8,32]{2,1,0:T(8,128)S(1)}, u32[]{:S(2)}, u32[]{:S(2)}) collective-permute-start(f32[1,8,32]{2,1,0:T(8,128)S(1)} %get-tuple-element.7), channel_id=1, source_target_pairs={{0,240},{4,244},{8,248},{12,252},{16,0},{20,4},{24,8},{28,12},{32,... | collective-permute-start | bytes 3080 | tf_op jit(solution)/shard_map/ppermute | solution.py:33
  367.4 20.7 %collective-permute-start.45 = (f32[1,8,32]{2,1,0:T(8,128)S(1)}, f32[1,8,32]{2,1,0:T(8,128)S(1)}, u32[]{:S(2)}, u32[]{:S(2)}) collective-permute-start(f32[1,8,32]{2,1,0:T(8,128)S(1)} %get-tuple-element.133), channel_id=1, source_target_pairs={{0,16},{4,20},{8,24},{12,28},{16,32},{20,36},{24,40},{28,44},{32,4... | collective-permute-start | bytes 3080 | tf_op jit(solution)/shard_map/ppermute | solution.py:33
  392.3 129.9 %collective-permute-start.74 = (bf16[16,1,8,32,64]{4,3,2,0,1:T(8,128)(2,1)}, bf16[16,1,8,32,64]{4,3,2,0,1:T(8,128)(2,1)S(1)}, u32[]{:S(2)}, u32[]{:S(2)}) collective-permute-start(bf16[16,1,8,32,64]{4,3,2,0,1:T(8,128)(2,1)} %get-tuple-element.73), channel_id=1, source_target_pairs={{0,12},{4,0},{8,4},{12,8},{16,28},{20,16},{24,20},{28,24},{32,44},... | collective-permute-start | bytes 1572872 | tf_op jit(solution)/shard_map/ppermute | solution.py:33
  394.2 151.6 %collective-permute-start.76 = (bf16[16,1,8,32,64]{4,3,2,0,1:T(8,128)(2,1)S(1)}, bf16[16,1,8,32,64]{4,3,2,0,1:T(8,128)(2,1)}, u32[]{:S(2)}, u32[]{:S(2)}) collective-permute-start(bf16[16,1,8,32,64]{4,3,2,0,1:T(8,128)(2,1)S(1)} %get-tuple-element.74), channel_id=1, source_target_pairs={{0,4},{4,8},{8,12},{12,0},{16,20},{20,24},{24,28},{28,16},{32,36},... | collective-permute-start | bytes 1572872 | tf_op jit(solution)/shard_map/ppermute | solution.py:33
  398.3 33.4 %collective-permute-start.61 = (f32[1,8,32]{2,1,0:T(8,128)S(1)}, f32[1,8,32]{2,1,0:T(8,128)S(1)}, u32[]{:S(2)}, u32[]{:S(2)}) collective-permute-start(f32[1,8,32]{2,1,0:T(8,128)S(1)} %get-tuple-element.50), channel_id=1, source_target_pairs={{0,240},{4,244},{8,248},{12,252},{16,0},{20,4},{24,8},{28,12},{32,... | collective-permute-start | bytes 3080 | tf_op jit(solution)/shard_map/ppermute | solution.py:33
  400.2 31.5 %collective-permute-start.68 = (f32[1,8,32]{2,1,0:T(8,128)S(1)}, f32[1,8,32]{2,1,0:T(8,128)S(1)}, u32[]{:S(2)}, u32[]{:S(2)}) collective-permute-start(f32[1,8,32]{2,1,0:T(8,128)S(1)} %get-tuple-element.126), channel_id=1, source_target_pairs={{0,16},{4,20},{8,24},{12,28},{16,32},{20,36},{24,40},{28,44},{32,4... | collective-permute-start | bytes 3080 | tf_op jit(solution)/shard_map/ppermute | solution.py:33
  433.0 21.4 %collective-permute-start.62 = (f32[1,8,32]{2,1,0:T(8,128)}, f32[1,8,32]{2,1,0:T(8,128)S(1)}, u32[]{:S(2)}, u32[]{:S(2)}) collective-permute-start(f32[1,8,32]{2,1,0:T(8,128)} %get-tuple-element.48), channel_id=1, source_target_pairs={{0,240},{4,244},{8,248},{12,252},{16,0},{20,4},{24,8},{28,12},{32,... | collective-permute-start | bytes 3080 | tf_op jit(solution)/shard_map/ppermute | solution.py:33
  434.9 20.1 %collective-permute-start.69 = (f32[1,8,32]{2,1,0:T(8,128)}, f32[1,8,32]{2,1,0:T(8,128)}, u32[]{:S(2)}, u32[]{:S(2)}) collective-permute-start(f32[1,8,32]{2,1,0:T(8,128)} %get-tuple-element.124), channel_id=1, source_target_pairs={{0,16},{4,20},{8,24},{12,28},{16,32},{20,36},{24,40},{28,44},{32,4... | collective-permute-start | bytes 3080 | tf_op jit(solution)/shard_map/ppermute | solution.py:33
  451.6 20.1 %collective-permute-start.46 = (f32[1,8,32]{2,1,0:T(8,128)}, f32[1,8,32]{2,1,0:T(8,128)}, u32[]{:S(2)}, u32[]{:S(2)}) collective-permute-start(f32[1,8,32]{2,1,0:T(8,128)} %get-tuple-element.131), channel_id=1, source_target_pairs={{0,16},{4,20},{8,24},{12,28},{16,32},{20,36},{24,40},{28,44},{32,4... | collective-permute-start | bytes 3080 | tf_op jit(solution)/shard_map/ppermute | solution.py:33
  456.4 15.3 %collective-permute-start.63 = (f32[1,8,32]{2,1,0:T(8,128)}, f32[1,8,32]{2,1,0:T(8,128)}, u32[]{:S(2)}, u32[]{:S(2)}) collective-permute-start(f32[1,8,32]{2,1,0:T(8,128)} %get-tuple-element.46), channel_id=1, source_target_pairs={{0,240},{4,244},{8,248},{12,252},{16,0},{20,4},{24,8},{28,12},{32,... | collective-permute-start | bytes 3080 | tf_op jit(solution)/shard_map/ppermute | solution.py:33
  473.0 18.5 %collective-permute-start.47 = (f32[1,8,32]{2,1,0:T(8,128)}, f32[1,8,32]{2,1,0:T(8,128)S(1)}, u32[]{:S(2)}, u32[]{:S(2)}) collective-permute-start(f32[1,8,32]{2,1,0:T(8,128)} %get-tuple-element.139), channel_id=1, source_target_pairs={{0,16},{4,20},{8,24},{12,28},{16,32},{20,36},{24,40},{28,44},{32,4... | collective-permute-start | bytes 3080 | tf_op jit(solution)/shard_map/ppermute | solution.py:33
  477.5 17.1 %collective-permute-start.64 = (f32[1,8,32]{2,1,0:T(8,128)}, f32[1,8,32]{2,1,0:T(8,128)}, u32[]{:S(2)}, u32[]{:S(2)}) collective-permute-start(f32[1,8,32]{2,1,0:T(8,128)} %get-tuple-element.44), channel_id=1, source_target_pairs={{0,240},{4,244},{8,248},{12,252},{16,0},{20,4},{24,8},{28,12},{32,... | collective-permute-start | bytes 3080 | tf_op jit(solution)/shard_map/ppermute | solution.py:33
  491.5 49.7 %collective-permute-start.22 = (bf16[16,1,32,8,64]{4,3,2,0,1:T(8,128)(2,1)}, bf16[16,1,32,8,64]{4,3,2,0,1:T(8,128)(2,1)}, u32[]{:S(2)}, u32[]{:S(2)}) collective-permute-start(bf16[16,1,32,8,64]{4,3,2,0,1:T(8,128)(2,1)} %get-tuple-element.75), channel_id=1, source_target_pairs={{0,12},{4,0},{8,4},{12,8},{16,28},{20,16},{24,20},{28,24},{32,44},... | collective-permute-start | bytes 1572872 | tf_op jit(solution)/shard_map/ppermute | solution.py:33
  510.7 18.2 %collective-permute-start.48 = (f32[1,8,32]{2,1,0:T(8,128)}, f32[1,8,32]{2,1,0:T(8,128)}, u32[]{:S(2)}, u32[]{:S(2)}) collective-permute-start(f32[1,8,32]{2,1,0:T(8,128)} %get-tuple-element.135), channel_id=1, source_target_pairs={{0,16},{4,20},{8,24},{12,28},{16,32},{20,36},{24,40},{28,44},{32,4... | collective-permute-start | bytes 3080 | tf_op jit(solution)/shard_map/ppermute | solution.py:33
  514.2 16.9 %collective-permute-start.66 = (f32[1,8,32]{2,1,0:T(8,128)}, f32[1,8,32]{2,1,0:T(8,128)}, u32[]{:S(2)}, u32[]{:S(2)}) collective-permute-start(f32[1,8,32]{2,1,0:T(8,128)} %get-tuple-element.40), channel_id=1, source_target_pairs={{0,240},{4,244},{8,248},{12,252},{16,0},{20,4},{24,8},{28,12},{32,... | collective-permute-start | bytes 3080 | tf_op jit(solution)/shard_map/ppermute | solution.py:33
  528.8 28.7 %collective-permute-start.25 = (bf16[16,1,32,8,64]{4,3,2,0,1:T(8,128)(2,1)S(1)}, bf16[16,1,32,8,64]{4,3,2,0,1:T(8,128)(2,1)}, u32[]{:S(2)}, u32[]{:S(2)}) collective-permute-start(bf16[16,1,32,8,64]{4,3,2,0,1:T(8,128)(2,1)S(1)} %get-tuple-element.76), channel_id=1, source_target_pairs={{0,4},{4,8},{8,12},{12,0},{16,20},{20,24},{24,28},{28,16},{32,36},... | collective-permute-start | bytes 1572872 | tf_op jit(solution)/shard_map/ppermute | solution.py:33
  531.1 16.4 %collective-permute-start.75 = (bf16[16,1,8,32,64]{4,3,2,0,1:T(8,128)(2,1)}, bf16[16,1,8,32,64]{4,3,2,0,1:T(8,128)(2,1)S(1)}, u32[]{:S(2)}, u32[]{:S(2)}) collective-permute-start(bf16[16,1,8,32,64]{4,3,2,0,1:T(8,128)(2,1)} %fusion.18), channel_id=1, source_target_pairs={{0,12},{4,0},{8,4},{12,8},{16,28},{20,16},{24,20},{28,24},{32,44},... | collective-permute-start | bytes 1572872 | tf_op jit(solution)/shard_map/ppermute | solution.py:33
  543.9 16.8 %collective-permute-start.23 = (bf16[16,1,32,8,64]{4,3,2,0,1:T(8,128)(2,1)S(1)}, bf16[16,1,32,8,64]{4,3,2,0,1:T(8,128)(2,1)S(1)}, u32[]{:S(2)}, u32[]{:S(2)}) collective-permute-start(bf16[16,1,32,8,64]{4,3,2,0,1:T(8,128)(2,1)S(1)} %fusion.23), channel_id=1, source_target_pairs={{0,12},{4,0},{8,4},{12,8},{16,28},{20,16},{24,20},{28,24},{32,44},... | collective-permute-start | bytes 1572872 | tf_op jit(solution)/shard_map/ppermute | solution.py:33
  551.9 23.9 %collective-permute-start.85 = (bf16[1,8,32,64]{3,2,1,0:T(8,128)(2,1)S(1)}, bf16[1,8,32,64]{3,2,1,0:T(8,128)(2,1)S(1)}, u32[]{:S(2)}, u32[]{:S(2)}) collective-permute-start(bf16[1,8,32,64]{3,2,1,0:T(8,128)(2,1)S(1)} %fusion.112), channel_id=1, source_target_pairs={{0,16},{4,20},{8,24},{12,28},{16,32},{20,36},{24,40},{28,44},{32,4... | collective-permute-start | bytes 98312 | tf_op jit(solution)/shard_map/ppermute | solution.py:33
  554.3 17.3 %collective-permute-start.77 = (bf16[1,8,32,64]{3,2,1,0:T(8,128)(2,1)S(1)}, bf16[1,8,32,64]{3,2,1,0:T(8,128)(2,1)S(1)}, u32[]{:S(2)}, u32[]{:S(2)}) collective-permute-start(bf16[1,8,32,64]{3,2,1,0:T(8,128)(2,1)S(1)} %fusion.111), channel_id=1, source_target_pairs={{0,240},{4,244},{8,248},{12,252},{16,0},{20,4},{24,8},{28,12},{32,... | collective-permute-start | bytes 98312 | tf_op jit(solution)/shard_map/ppermute | solution.py:33
  567.3 18.2 %collective-permute-start.49 = (bf16[1,32,8,64]{3,2,1,0:T(8,128)(2,1)S(1)}, bf16[1,32,8,64]{3,2,1,0:T(8,128)(2,1)S(1)}, u32[]{:S(2)}, u32[]{:S(2)}) collective-permute-start(bf16[1,32,8,64]{3,2,1,0:T(8,128)(2,1)S(1)} %get-tuple-element.102), channel_id=1, source_target_pairs={{0,16},{4,20},{8,24},{12,28},{16,32},{20,36},{24,40},{28,44},{32,4... | collective-permute-start | bytes 98312 | tf_op jit(solution)/shard_map/ppermute | solution.py:33
  655.9 53.1 %collective-permute-start.41 = (bf16[1,32,8,64]{3,2,1,0:T(8,128)(2,1)S(1)}, bf16[1,32,8,64]{3,2,1,0:T(8,128)(2,1)S(1)}, u32[]{:S(2)}, u32[]{:S(2)}) collective-permute-start(bf16[1,32,8,64]{3,2,1,0:T(8,128)(2,1)S(1)} %get-tuple-element.89), channel_id=1, source_target_pairs={{0,240},{4,244},{8,248},{12,252},{16,0},{20,4},{24,8},{28,12},{32,... | collective-permute-start | bytes 98312 | tf_op jit(solution)/shard_map/ppermute | solution.py:33
  657.8 51.2 %collective-permute-start.55 = (bf16[1,32,8,64]{3,2,1,0:T(8,128)(2,1)S(1)}, bf16[1,32,8,64]{3,2,1,0:T(8,128)(2,1)S(1)}, u32[]{:S(2)}, u32[]{:S(2)}) collective-permute-start(bf16[1,32,8,64]{3,2,1,0:T(8,128)(2,1)S(1)} %get-tuple-element.90), channel_id=1, source_target_pairs={{0,16},{4,20},{8,24},{12,28},{16,32},{20,36},{24,40},{28,44},{32,4... | collective-permute-start | bytes 98312 | tf_op jit(solution)/shard_map/ppermute | solution.py:33
  (174 other events, 5117.7 us)
